TPU v7x, 256 devices: a whole 4x4x8 slice. The times are simulated.
256 devices in a mesh: dp: 32 (over x, z_hi, y), mp: 8 (over z_lo, core).
Axes of the slice: x: 4, y: 4, z: 8 (z_hi: 2, z_lo: 4; z = z_hi * 4 + z_lo), core: 2. Of those that a mesh axis runs over, the one named last changes fastest.
Arguments:
- store_rows: bfloat16 [8192, 8192], P('dp', 'mp'), may hold values from -6 to 6
- source_shard: int32 [1024], replicated, may hold values from 0 to 31, as said below
- source_row: int32 [1024], replicated, may hold values from 0 to 255
- state_len: int32 [32], replicated, may hold values from 1 to 64, 1024 in all
- visits: int32 [32], replicated, may hold values from 1 to 4095
- gain: bfloat16 [8192], P('mp'), may hold values from 0.5 to 1.5
- w_gate: bfloat16 [8192, 22016], P('mp', 'dp'), may hold values from -0.0625 to 0.0625
- w_up: bfloat16 [8192, 22016], P('mp', 'dp'), may hold values from -0.0625 to 0.0625
- w_down: bfloat16 [22016, 8192], P('dp', 'mp'), may hold values from -0.0390625 to 0.0390625
- upstream: bfloat16 [1024, 8192], P(None, 'mp'), may hold values from -0.375 to 0.375
Outputs:
- layer_out: bfloat16 [1024, 8192], P('dp', 'mp')
- grad_gate: bfloat16 [8192, 22016], P('mp', 'dp')
- grad_up: bfloat16 [8192, 22016], P('mp', 'dp')
- grad_down: bfloat16 [22016, 8192], P('dp', 'mp')
Inputs may be any that keep to these rules, and one draw needn't show every extreme that they name: `source_shard`: block b holds training rows b * 32 to (b + 1) * 32 - 1. No shard is named more than 4 times in one block nor more than 128 times in all; one shard, drawn from the seed, is named exactly 4 times in every block. `state_len`: the lengths sum to 1024.
All inputs are finite; a program needn't handle non-finite values.
Results may differ from a plain program's by a relative error of at most 0.017.
Values may be sent and summed in bfloat16 or wider, within the bound.
No kernel may reach another device: no remote copies, remote signals or barrier semaphores. Data moves between devices by JAX's collectives and lax.ppermute only.
A program may use at most 64 MiB of HBM per device.

v0:
```python
import jax
import jax.numpy as jnp
from jax import lax
from jax.sharding import Mesh
from jax.sharding import PartitionSpec as P

D = 8192
epsilon = 1e-05
DP = ("x", "zh", "y")
MP = ("zl", "c")


def shards(
    store_rows, source_shard, source_row, state_len, visits, gain, w_gate, w_up, w_down, upstream
):
    f32, bf16 = (jnp.float32, jnp.bfloat16)
    count_dp = 1
    for name in DP:
        count_dp *= lax.axis_size(name)
    index_dp = lax.axis_index(DP)
    total_rows = source_shard.shape[0]
    block_rows = total_rows // count_dp
    pair_cap = max(block_rows // 8, 1)
    store_dev = store_rows.shape[0]
    hidden_dev = w_gate.shape[1]
    shard = source_shard.reshape(count_dp, block_rows)
    srow = source_row.reshape(count_dp, block_rows)
    same = shard[:, :, None] == shard[:, None, :]
    t_ids = jnp.arange(block_rows, dtype=jnp.int32)
    earlier = t_ids[None, :] < t_ids[:, None]
    rank = jnp.sum((same & earlier[None]).astype(jnp.int32), axis=2)
    owned = shard == index_dp
    slots = jnp.arange(pair_cap, dtype=jnp.int32)
    hit = owned[:, :, None] & (rank[:, :, None] == slots[None, None, :])
    slot_row = jnp.sum(jnp.where(hit, srow[:, :, None] + 1, 0), axis=1) - 1
    pick_out = (
        slot_row.reshape(count_dp * pair_cap)[:, None]
        == jnp.arange(store_dev, dtype=jnp.int32)[None, :]
    ).astype(bf16)
    outgoing = jnp.dot(pick_out, store_rows, preferred_element_type=f32).astype(bf16)
    received = lax.all_to_all(outgoing, DP, 0, 0, tiled=True)
    my_shard = lax.dynamic_index_in_dim(shard, index_dp, 0, keepdims=False)
    my_rank = lax.dynamic_index_in_dim(rank, index_dp, 0, keepdims=False)
    pick_in = (
        (my_shard * pair_cap + my_rank)[:, None]
        == jnp.arange(count_dp * pair_cap, dtype=jnp.int32)[None, :]
    ).astype(bf16)
    own_rows = jnp.dot(pick_in, received, preferred_element_type=f32).astype(bf16)
    train_rows = own_rows
    for name in reversed(DP):
        train_rows = lax.all_gather(train_rows, name, axis=0, tiled=True)
    rows_float = train_rows.astype(f32)
    squares = jnp.sum(rows_float * rows_float, axis=1)
    scaled = (rows_float * gain.astype(f32)[None, :]).astype(bf16)
    gate_term = jnp.dot(scaled, w_gate, preferred_element_type=f32)
    up_term = jnp.dot(scaled, w_up, preferred_element_type=f32)
    packed = jnp.concatenate([gate_term, up_term, squares[:, None]], axis=1)
    total = lax.psum(packed, MP)
    gate_total = total[:, :hidden_dev]
    up_total = total[:, hidden_dev : 2 * hidden_dev]
    square_total = total[:, 2 * hidden_dev]
    inverse = lax.rsqrt(square_total / D + epsilon)
    gate_all = inverse[:, None] * gate_total
    up_all = inverse[:, None] * up_total
    hidden_all = (jax.nn.silu(gate_all) * up_all).astype(bf16)
    down_part = jnp.dot(hidden_all, w_down, preferred_element_type=f32).astype(bf16)
    down_in = lax.all_to_all(down_part, DP, 0, 0, tiled=True)
    down_block = jnp.sum(
        down_in.reshape(count_dp, block_rows, down_in.shape[1]).astype(f32), axis=0
    )
    layer_out = (own_rows.astype(f32) + down_block).astype(bf16)
    row_ids = jnp.arange(total_rows, dtype=jnp.int32)
    ends = jnp.cumsum(state_len)
    starts = ends - state_len
    member = ((row_ids[:, None] >= starts[None, :]) & (row_ids[:, None] < ends[None, :])).astype(
        f32
    )
    importance = jnp.log1p(visits.astype(f32))
    per_state = total_rows * importance / (state_len.astype(f32) * jnp.sum(importance))
    row_weight = jnp.sum(member * per_state[None, :], axis=1)
    out_grad = (upstream.astype(f32) * row_weight[:, None]).astype(bf16)
    grad_down = lax.dot_general(
        hidden_all, out_grad, (((0,), (0,)), ((), ())), preferred_element_type=f32
    ).astype(bf16)
    hidden_term = lax.dot_general(
        out_grad, w_down, (((1,), (1,)), ((), ())), preferred_element_type=f32
    ).astype(bf16)
    grad_hidden = lax.psum(hidden_term, MP).astype(f32)
    sigmoid_gate = jax.nn.sigmoid(gate_all)
    gate_delta = (
        inverse[:, None]
        * grad_hidden
        * up_all
        * sigmoid_gate
        * (1.0 + gate_all * (1.0 - sigmoid_gate))
    ).astype(bf16)
    up_delta = (inverse[:, None] * grad_hidden * gate_all * sigmoid_gate).astype(bf16)
    grad_gate = lax.dot_general(
        scaled, gate_delta, (((0,), (0,)), ((), ())), preferred_element_type=f32
    ).astype(bf16)
    grad_up = lax.dot_general(
        scaled, up_delta, (((0,), (0,)), ((), ())), preferred_element_type=f32
    ).astype(bf16)
    return (layer_out, grad_gate, grad_up, grad_down)


def solution(mesh):
    sizes = dict(zip(mesh.axis_names, mesh.devices.shape))
    count_mp = sizes["mp"]
    count_dp = sizes["dp"]
    zh = 2
    y = 4
    x = count_dp // (zh * y)
    c = 2
    zl = count_mp // c
    view = Mesh(mesh.devices.reshape(x, zh, y, zl, c), DP + MP)
    in_specs = (P(DP, MP), P(), P(), P(), P(), P(MP), P(MP, DP), P(MP, DP), P(DP, MP), P(None, MP))
    out_specs = (P(DP, MP), P(MP, DP), P(MP, DP), P(DP, MP))
    return jax.shard_map(shards, mesh=view, in_specs=in_specs, out_specs=out_specs, check_vma=False)
```

profile of v0, /device:TPU:2, one launch (start us, length us, event | category | flops | bytes accessed | tf_op | source)
XLA Modules:
  0.0 380.9 jit_solution(1981180116354993840)
XLA Ops:
  7.2 0.0 copy-start
  7.2 0.0 copy-start.5
  7.2 0.9 reshape.93
  8.1 0.8 convert_reduce_fusion.1
  8.9 0.7 broadcast_add_fusion
  9.6 0.1 add.70
  9.6 0.1 select_reduce_fusion.1
  9.8 0.1 copy.16
  9.9 0.1 sub.13
  10.0 1.3 convolution_convert_fusion.5
  11.3 0.0 copy-start.8
  11.3 0.8 all_to_all.14
  12.1 14.2 %all-to-all-start = ((bf16[32,4,1024]{2,1,0:T(4,128)(2,1)}), bf16[32,4,1024]{2,1,0:T(4,128)(2,1)S(1)}, u32[]{:S(2)}, u32[]{:S(2)}) async-start(bf16[32,4,1024]{2,1,0:T(4,128)(2,1)} %all_to_all.14), calls=%async_computation | async-start | bytes 524288 | tf_op jit(solution)/shard_map/all_to_all | solution.py:41
  26.4 0.0 all-gather.2.cloned.1.call-start
  26.5 12.0 %all-to-all-done = bf16[32,4,1024]{2,1,0:T(4,128)(2,1)S(1)} async-done(((bf16[32,4,1024]{2,1,0:T(4,128)(2,1)}), bf16[32,4,1024]{2,1,0:T(4,128)(2,1)S(1)}, u32[]{:S(2)}, u32[]{:S(2)}) %all-to-all-start) | async-done | bytes 262176 | tf_op jit(solution)/shard_map/all_to_all | solution.py:41
  38.4 0.1 all_to_all.16
  38.5 0.2 convolution_convert_fusion.6
  38.7 0.0 copy-start.4
  38.7 0.6 copy-done.4
  39.4 12.2 %all_gather.9 = bf16[128,1024]{1,0:T(8,128)(2,1)S(1)} all-gather(bf16[32,1024]{1,0:T(8,128)(2,1)S(1)} %convolution_convert_fusion.6), channel_id=1, replica_groups=mesh['x'=4,'zh'=2,'y'=4,'zl'=4,'c'=2] {'y'}, dimensions={0}, use_global_device_ids=true | all-gather | bytes 327680 | tf_op jit(solution)/shard_map/all_gather | solution.py:51
  51.6 13.8 %all_gather.10 = bf16[256,1024]{1,0:T(8,128)(2,1)} all-gather(bf16[128,1024]{1,0:T(8,128)(2,1)S(1)} %all_gather.9), channel_id=1, replica_groups=mesh['x'=4,'zh'=2,'y'=4,'zl'=4,'c'=2] {'zh'}, dimensions={0}, use_global_device_ids=true | all-gather | bytes 786432 | tf_op jit(solution)/shard_map/all_gather | solution.py:51
  65.4 0.0 all-gather.2.cloned.1.call-update
  65.5 0.0 all-reduce.3.cloned.1.call-start
  65.5 0.0 copy-done.5
  65.5 28.7 %all-gather.2.cloned.1.call-done = bf16[1024,1024]{1,0:T(8,128)(2,1)} async-done(((bf16[256,1024]{1,0:T(8,128)(2,1)}), bf16[1024,1024]{1,0:T(8,128)(2,1)}) %all-gather.2.cloned.1.call-update) | async-done | bytes 2097168 | tf_op jit(solution)/shard_map/all_gather | solution.py:51
  94.3 2.1 fusion.1
  96.3 0.0 copy-done.8
  96.4 0.0 copy-start.1
  96.4 0.0 copy-start.9
  96.4 3.4 fusion.4
  99.8 0.0 copy-done.1
  99.8 0.0 copy-done.9
  99.8 1.7 fusion.6
  101.5 3.0 pad_maximum_fusion
  104.5 0.0 copy-start.6
  104.5 0.0 all-reduce.3.cloned.1.call-update
  104.5 0.6 copy-done.6
  105.2 0.1 copy.17
  105.2 0.1 reduce-window.8
  105.3 0.1 reduce
  105.4 137.3 %all-reduce.3.cloned.1.call-done = f32[1024,1377]{0,1:T(8,128)} async-done(((f32[1024,1377]{0,1:T(8,128)}), f32[1024,1377]{0,1:T(8,128)}) %all-reduce.3.cloned.1.call-update) | async-done | bytes 5640208 | tf_op jit(solution)/shard_map/psum | solution.py:58
  242.8 0.8 fusion.13
  243.5 3.5 multiply_convert_fusion.3
  247.0 0.0 copy-done
  247.0 0.0 copy-start.3
  247.0 3.2 convolution_convert_fusion
  250.2 0.0 copy-done.3
  250.2 10.0 %all-to-all-start.1 = ((bf16[32,32,1024]{2,1,0:T(8,128)(2,1)}), bf16[32,32,1024]{2,1,0:T(8,128)(2,1)S(1)}, u32[]{:S(2)}, u32[]{:S(2)}) async-start(bf16[32,32,1024]{2,1,0:T(8,128)(2,1)} %bitcast.14), calls=%async_computation.1 | async-start | bytes 4194304 | tf_op jit(solution)/shard_map/all_to_all | solution.py:67
  260.2 0.2 all-reduce.5.cloned.1.call-start
  260.5 0.0 copy-done.7
  260.5 0.6 fusion.14
  261.1 0.7 multiply_divide_fusion
  261.8 0.1 select_reduce_fusion
  261.9 4.4 %convolution_convert_fusion.4 = bf16[1024,688]{0,1:T(8,128)(2,1)} fusion(bf16[688,1024]{1,0:T(8,128)(2,1)S(1)} %copy-done, bf16[1024,1024]{1,0:T(8,128)(2,1)} %param.19, f32[1024]{0:T(1024)S(1)} %select_reduce_fusion), kind=kOutput, calls=%fused_computation.18 | convolution fusion | flops 1446690816 | bytes 4919296 | tf_op jit(solution)/shard_map/dot_general | solution.py:85
  266.3 0.0 all-reduce.5.cloned.1.call-update
  266.3 4.8 %convolution_convert_fusion.3 = bf16[688,1024]{1,0:T(8,128)(2,1)} fusion(bf16[1024,688]{0,1:T(8,128)(2,1)} %copy-done.3, bf16[1024,1024]{1,0:T(8,128)(2,1)} %param.19, f32[1024]{0:T(1024)S(1)} %select_reduce_fusion), kind=kOutput, calls=%fused_computation.17 | convolution fusion | flops 1446690816 | bytes 4919296 | tf_op jit(solution)/shard_map/dot_general | solution.py:82
  271.1 89.1 %all-reduce.5.cloned.1.call-done = bf16[1024,688]{0,1:T(8,128)(2,1)} async-done(((bf16[1024,688]{0,1:T(8,128)(2,1)}), bf16[1024,688]{0,1:T(8,128)(2,1)}) %all-reduce.5.cloned.1.call-update) | async-done | bytes 1409040 | tf_op jit(solution)/shard_map/psum | solution.py:88
  360.2 6.1 %convolution_convert_fusion.1 = bf16[1024,688]{0,1:T(8,128)(2,1)} fusion(bf16[1024,688]{0,1:T(8,128)(2,1)} %all-reduce.5.cloned.1.call-done, f32[1024,1377]{0,1:T(8,128)} %all-reduce.3.cloned.1.call-done, f32[1024]{0:T(1024)S(1)} %bitcast.17, bf16[1024,1024]{1,0:T(8,128)(2,1)} %all-gather.2.cloned.1.call-done, f32[1024]{0:T(1024)S(1)} %convert_element_type.74), kind=kOutput, calls=%fused_computation.15 | convolution fusion | flops 1453031424 | bytes 7741440 | tf_op jit(solution)/shard_map/dot_general | solution.py:101
  366.3 0.0 copy-done.2
  366.3 0.0 copy-done.10
  366.3 6.3 %convolution_convert_fusion.2 = bf16[1024,688]{0,1:T(8,128)(2,1)} fusion(bf16[1024,688]{0,1:T(8,128)(2,1)S(1)} %copy-done.10, f32[1024,1377]{0,1:T(8,128)} %all-reduce.3.cloned.1.call-done, f32[1024]{0:T(1024)S(1)} %bitcast.18, bf16[1024,1024]{1,0:T(8,128)(2,1)S(1)} %copy-done.2, f32[1024]{0:T(1024)S(1)} %convert_element_type.74), kind=kOutput, calls=%fused_computation.16 | convolution fusion | flops 1456553984 | bytes 10559488 | tf_op jit(solution)/shard_map/dot_general | solution.py:98
  372.6 0.0 all-to-all-done.1
  372.6 0.4 convert_reduce_fusion
  372.9 1.5 add_convert_fusion
  (9 shorter events, 0.1 us)
Async XLA Ops:
  7.2 239.8 %copy-start = (bf16[688,1024]{1,0:T(8,128)(2,1)S(1)}, bf16[688,1024]{1,0:T(8,128)(2,1)}, u32[]{:S(2)}) copy-start(bf16[688,1024]{1,0:T(8,128)(2,1)} %param.18) | copy-start | bytes 4227076
  7.2 58.3 %copy-start.5 = (bf16[1024]{0:T(1024)(128)(2,1)S(1)}, bf16[1024]{0:T(1024)(128)(2,1)}, u32[]{:S(2)}) copy-start(bf16[1024]{0:T(1024)(128)(2,1)} %param.15) | copy-start | bytes 6148
  11.3 85.0 %copy-start.8 = (bf16[1024,688]{0,1:T(8,128)(2,1)S(1)}, bf16[1024,688]{0,1:T(8,128)(2,1)}, u32[]{:S(2)}) copy-start(bf16[1024,688]{0,1:T(8,128)(2,1)} %param.17) | copy-start | bytes 4227076
  12.1 26.3 %all-to-all-start = ((bf16[32,4,1024]{2,1,0:T(4,128)(2,1)}), bf16[32,4,1024]{2,1,0:T(4,128)(2,1)S(1)}, u32[]{:S(2)}, u32[]{:S(2)}) async-start(bf16[32,4,1024]{2,1,0:T(4,128)(2,1)} %all_to_all.14), calls=%async_computation | async-start | bytes 524288 | tf_op jit(solution)/shard_map/all_to_all | solution.py:41
  26.4 67.9 %all-gather.2.cloned.1.call-start = ((), (), s32[]{:S(2)}) async-start(), calls=%async_computation.2 | async-start | bytes 2621440 | tf_op jit(solution)/shard_map/all_gather | solution.py:51
  38.7 0.6 copy-start.4
  65.5 177.3 %all-reduce.3.cloned.1.call-start = ((), (), s32[]{:S(2)}) async-start(), calls=%async_computation.3 | async-start | bytes 11337728 | tf_op jit(solution)/shard_map/psum | solution.py:58
  96.4 3.4 copy-start.1
  96.4 3.4 copy-start.9
  104.5 0.7 copy-start.6
  247.0 3.2 copy-start.3
  250.2 10.3 %copy-start.7 = (s32[32]{0:T(128)S(1)}, s32[32]{0:T(128)}, u32[]{:S(2)}) copy-start(s32[32]{0:T(128)} %param.14) | copy-start | bytes 388
  250.2 122.4 %all-to-all-start.1 = ((bf16[32,32,1024]{2,1,0:T(8,128)(2,1)}), bf16[32,32,1024]{2,1,0:T(8,128)(2,1)S(1)}, u32[]{:S(2)}, u32[]{:S(2)}) async-start(bf16[32,32,1024]{2,1,0:T(8,128)(2,1)} %bitcast.14), calls=%async_computation.1 | async-start | bytes 4194304 | tf_op jit(solution)/shard_map/all_to_all | solution.py:67
  260.2 100.0 %all-reduce.5.cloned.1.call-start = ((), (), s32[]{:S(2)}) async-start(), calls=%async_computation.4 | async-start | bytes 2818048 | tf_op jit(solution)/shard_map/psum | solution.py:88
  360.2 6.1 %copy-start.2 = (bf16[1024,1024]{1,0:T(8,128)(2,1)S(1)}, bf16[1024,1024]{1,0:T(8,128)(2,1)}, u32[]{:S(2)}) copy-start(bf16[1024,1024]{1,0:T(8,128)(2,1)} %all-gather.2.cloned.1.call-done) | copy-start | bytes 6291460
  360.2 6.1 %copy-start.10 = (bf16[1024,688]{0,1:T(8,128)(2,1)S(1)}, bf16[1024,688]{0,1:T(8,128)(2,1)}, u32[]{:S(2)}) copy-start(bf16[1024,688]{0,1:T(8,128)(2,1)} %all-reduce.5.cloned.1.call-done) | copy-start | bytes 4227076
Sparse Core Ops, SparseCore 0:
  65.6 28.6 all-gather.1
  104.6 138.0 all-reduce.2
  266.4 93.7 all-reduce.4
where the time goes:
time: 382 us; the launch traced here: 381 us
  waiting for transfers between devices  267 us (70%)
  matrix products  31.4 us (8%)
  blocking collectives  26.1 us (7%)
  starting transfers between devices  24.6 us (6%)
  other arithmetic  14.4 us (4%)
  between operations  14 us (4%)
    psum x1, waiting for transfers between devices, shards(): total = lax.psum(packed, MP)  137 us
    psum x1, waiting for transfers between devices, shards(): grad_hidden = lax.psum(hidden_term, MP).astype(f32)  89.1 us
    all_gather x1, waiting for transfers between devices, shards(): train_rows = lax.all_gather(train_rows, name, axis=0, tiled=True)  28.7 us
    all_gather x2, blocking collectives, shards(): train_rows = lax.all_gather(train_rows, name, axis=0, tiled=True)  26.1 us
    all_to_all x1, starting transfers between devices, shards(): received = lax.all_to_all(outgoing, DP, 0, 0, tiled=True)  14.2 us
    all_to_all x1, waiting for transfers between devices, shards(): received = lax.all_to_all(outgoing, DP, 0, 0, tiled=True)  12 us
    all_to_all x1, starting transfers between devices, shards(): down_in = lax.all_to_all(down_part, DP, 0, 0, tiled=True)  10 us
  transfers between devices with their start and end apart: 5, of which 4 were waited for; matrix products, arithmetic and copies ran while one was open for 6% of the time, Pallas kernels for 0%

commit v1 on v0

--- a/solution.py
+++ b/solution.py
@@ -48,7 +48,10 @@
     own_rows = jnp.dot(pick_in, received, preferred_element_type=f32).astype(bf16)
     train_rows = own_rows
     for name in reversed(DP):
-        train_rows = lax.all_gather(train_rows, name, axis=0, tiled=True)
+        train_rows = jnp.concatenate(
+            jax.lax.all_to_all(jnp.stack(jax.lax.axis_size(name) * [train_rows]), name, 0, 0),
+            axis=0,
+        )
     rows_float = train_rows.astype(f32)
     squares = jnp.sum(rows_float * rows_float, axis=1)
     scaled = (rows_float * gain.astype(f32)[None, :]).astype(bf16)

time: 382 us -> 377 us (0.987)
  waiting for transfers between devices: 267 us -> 257 us
  starting transfers between devices: 24.6 us -> 29.6 us
    all_gather x1 -> x0, waiting for transfers between devices: 28.7 us -> none  [shards(): train_rows = lax.all_gather(train_rows, name, axis=0, tiled=True)]
    all_to_all x0 -> x2, blocking collectives: none -> 26.9 us  [shards(): jax.lax.all_to_all(jnp.stack(jax.lax.axis_size(name) * [train_rows]), nam...]
    all_gather x2 -> x0, blocking collectives: 26.1 us -> none  [shards(): train_rows = lax.all_gather(train_rows, name, axis=0, tiled=True)]
    all_to_all x0 -> x1, waiting for transfers between devices: none -> 17.4 us  [shards(): jax.lax.all_to_all(jnp.stack(jax.lax.axis_size(name) * [train_rows]), nam...]
    all_to_all x0 -> x1, starting transfers between devices: none -> 5.11 us  [shards(): jax.lax.all_to_all(jnp.stack(jax.lax.axis_size(name) * [train_rows]), nam...]
where the time goes in v1:
time: 377 us; the launch traced here: 376 us
  waiting for transfers between devices  257 us (68%)
  starting transfers between devices  29.6 us (8%)
  matrix products  29.3 us (8%)
  blocking collectives  26.9 us (7%)
  between operations  14.2 us (4%)
  other arithmetic  13.4 us (4%)
  local copies, waits for them, and re-layouts  5.04 us (1%)
    psum x1, waiting for transfers between devices, shards(): total = lax.psum(packed, MP)  139 us
    psum x1, waiting for transfers between devices, shards(): grad_hidden = lax.psum(hidden_term, MP).astype(f32)  88.9 us
    all_to_all x2, blocking collectives, shards(): jax.lax.all_to_all(jnp.stack(jax.lax.axis_size(name) * [train_rows]), nam...  26.9 us
    all_to_all x1, waiting for transfers between devices, shards(): jax.lax.all_to_all(jnp.stack(jax.lax.axis_size(name) * [train_rows]), nam...  17.4 us
    all_to_all x1, starting transfers between devices, shards(): received = lax.all_to_all(outgoing, DP, 0, 0, tiled=True)  14.2 us
    all_to_all x1, waiting for transfers between devices, shards(): received = lax.all_to_all(outgoing, DP, 0, 0, tiled=True)  12 us
    all_to_all x1, starting transfers between devices, shards(): down_in = lax.all_to_all(down_part, DP, 0, 0, tiled=True)  10 us
  transfers between devices with their start and end apart: 5, of which 4 were waited for; matrix products, arithmetic and copies ran while one was open for 6% of the time, Pallas kernels for 0%

profile of v1, /device:TPU:2, one launch (start us, length us, event | category | flops | bytes accessed | tf_op | source)
XLA Modules:
  0.0 375.8 jit_solution(3873781843032737663)
XLA Ops:
  7.2 0.0 copy-start
  7.2 0.9 reshape.102
  8.1 0.8 convert_reduce_fusion.1
  8.9 0.7 broadcast_add_fusion
  9.6 0.1 add.70
  9.6 0.1 select_reduce_fusion.1
  9.8 0.1 copy.16
  9.9 0.1 sub.13
  10.0 1.3 convolution_convert_fusion.5
  11.3 0.8 all_to_all.23
  12.1 14.2 %all-to-all-start = ((bf16[32,4,1024]{2,1,0:T(4,128)(2,1)}), bf16[32,4,1024]{2,1,0:T(4,128)(2,1)S(1)}, u32[]{:S(2)}, u32[]{:S(2)}) async-start(bf16[32,4,1024]{2,1,0:T(4,128)(2,1)} %all_to_all.23), calls=%async_computation | async-start | bytes 524288 | tf_op jit(solution)/shard_map/all_to_all | solution.py:41
  26.4 12.0 %all-to-all-done = bf16[32,4,1024]{2,1,0:T(4,128)(2,1)S(1)} async-done(((bf16[32,4,1024]{2,1,0:T(4,128)(2,1)}), bf16[32,4,1024]{2,1,0:T(4,128)(2,1)S(1)}, u32[]{:S(2)}, u32[]{:S(2)}) %all-to-all-start) | async-done | bytes 262176 | tf_op jit(solution)/shard_map/all_to_all | solution.py:41
  38.4 0.1 all_to_all.25
  38.5 0.2 convolution_convert_fusion.6
  38.7 0.0 copy-start.4
  38.7 9.1 %all_to_all.36 = bf16[4,32,1024]{2,1,0:T(8,128)(2,1)S(1)} all-to-all(bf16[4,32,1024]{2,1,0:T(8,128)(2,1)S(1)} %stack.6), channel_id=1, replica_groups=mesh['x'=4,'zh'=2,'y'=4,'zl'=4,'c'=2] {'y'}, dimensions={0} | all-to-all | bytes 524288 | tf_op jit(solution)/shard_map/all_to_all | solution.py:52
  47.8 0.0 copy-done.4
  47.9 17.8 %all_to_all.37 = bf16[2,128,1024]{2,1,0:T(8,128)(2,1)S(1)} all-to-all(bf16[2,128,1024]{2,1,0:T(8,128)(2,1)S(1)} %pad_maximum_fusion.1), channel_id=1, replica_groups=mesh['x'=4,'zh'=2,'y'=4,'zl'=4,'c'=2] {'zh'}, dimensions={0} | all-to-all | bytes 1048576 | tf_op jit(solution)/shard_map/all_to_all | solution.py:52
  65.7 0.0 copy-start.5
  65.7 1.6 stack.15
  67.3 5.1 %all-to-all-start.3 = ((bf16[4,256,1024]{2,1,0:T(8,128)(2,1)}), bf16[4,256,1024]{2,1,0:T(8,128)(2,1)S(1)}, u32[]{:S(2)}, u32[]{:S(2)}) async-start(bf16[4,256,1024]{2,1,0:T(8,128)(2,1)} %stack.15), calls=%async_computation.3 | async-start | bytes 4194304 | tf_op jit(solution)/shard_map/all_to_all | solution.py:52
  72.4 0.0 all-reduce.3.cloned.1.call-start
  72.4 0.0 copy-done.5
  72.4 17.4 %all-to-all-done.3 = bf16[4,256,1024]{2,1,0:T(8,128)(2,1)S(1)} async-done(((bf16[4,256,1024]{2,1,0:T(8,128)(2,1)}), bf16[4,256,1024]{2,1,0:T(8,128)(2,1)S(1)}, u32[]{:S(2)}, u32[]{:S(2)}) %all-to-all-start.3) | async-done | bytes 2097184 | tf_op jit(solution)/shard_map/all_to_all | solution.py:52
  89.8 0.0 copy-start.8
  89.8 0.5 fusion
  90.4 0.8 copy-done.8
  91.2 0.0 copy-start.1
  91.2 0.0 copy-start.9
  91.2 1.7 fusion.10
  92.9 0.0 copy-done.1
  92.9 0.4 copy-done.9
  93.3 1.7 fusion.11
  95.0 0.5 multiply_reduce_fusion
  95.5 3.0 pad_maximum_fusion
  98.5 0.0 all-reduce.3.cloned.1.call-update
  98.5 139.0 %all-reduce.3.cloned.1.call-done = f32[1024,1377]{0,1:T(8,128)} async-done(((f32[1024,1377]{0,1:T(8,128)}), f32[1024,1377]{0,1:T(8,128)}) %all-reduce.3.cloned.1.call-update) | async-done | bytes 5640208 | tf_op jit(solution)/shard_map/psum | solution.py:61
  237.5 0.8 fusion.6
  238.3 3.5 multiply_convert_fusion.3
  241.8 0.0 copy-done
  241.8 0.0 copy-start.3
  241.8 3.2 convolution_convert_fusion
  245.0 0.0 copy-done.3
  245.0 10.0 %all-to-all-start.4 = ((bf16[32,32,1024]{2,1,0:T(8,128)(2,1)}), bf16[32,32,1024]{2,1,0:T(8,128)(2,1)S(1)}, u32[]{:S(2)}, u32[]{:S(2)}) async-start(bf16[32,32,1024]{2,1,0:T(8,128)(2,1)} %bitcast.28), calls=%async_computation.4 | async-start | bytes 4194304 | tf_op jit(solution)/shard_map/all_to_all | solution.py:70
  255.0 0.2 all-reduce.5.cloned.1.call-start
  255.2 0.0 copy-done.6
  255.3 0.1 copy.17
  255.3 0.1 reduce-window.8
  255.4 0.1 reduce.1
  255.5 0.0 copy-done.7
  255.5 0.6 fusion.7
  256.1 0.7 multiply_divide_fusion
  256.8 0.1 select_reduce_fusion
  256.9 4.4 %convolution_convert_fusion.4 = bf16[1024,688]{0,1:T(8,128)(2,1)} fusion(bf16[688,1024]{1,0:T(8,128)(2,1)S(1)} %copy-done, bf16[1024,1024]{1,0:T(8,128)(2,1)} %param.19, f32[1024]{0:T(1024)S(1)} %select_reduce_fusion), kind=kOutput, calls=%fused_computation.17 | convolution fusion | flops 1446690816 | bytes 4919296 | tf_op jit(solution)/shard_map/dot_general | solution.py:88
  261.3 0.0 all-reduce.5.cloned.1.call-update
  261.3 4.8 %convolution_convert_fusion.3 = bf16[688,1024]{1,0:T(8,128)(2,1)} fusion(bf16[1024,688]{0,1:T(8,128)(2,1)} %copy-done.3, bf16[1024,1024]{1,0:T(8,128)(2,1)} %param.19, f32[1024]{0:T(1024)S(1)} %select_reduce_fusion), kind=kOutput, calls=%fused_computation.16 | convolution fusion | flops 1446690816 | bytes 4919296 | tf_op jit(solution)/shard_map/dot_general | solution.py:85
  266.2 88.9 %all-reduce.5.cloned.1.call-done = bf16[1024,688]{0,1:T(8,128)(2,1)} async-done(((bf16[1024,688]{0,1:T(8,128)(2,1)}), bf16[1024,688]{0,1:T(8,128)(2,1)}) %all-reduce.5.cloned.1.call-update) | async-done | bytes 1409040 | tf_op jit(solution)/shard_map/psum | solution.py:91
  355.0 5.9 %convolution_convert_fusion.1 = bf16[1024,688]{0,1:T(8,128)(2,1)} fusion(bf16[1024,1024]{1,0:T(8,128)(2,1)} %copy-done.1, bf16[1024,688]{0,1:T(8,128)(2,1)} %all-reduce.5.cloned.1.call-done, f32[1024,1377]{0,1:T(8,128)} %all-reduce.3.cloned.1.call-done, f32[1024]{0:T(1024)S(1)} %bitcast.32), kind=kOutput, calls=%fused_computation.14 | convolution fusion | flops 1449885696 | bytes 7737344 | tf_op jit(solution)/shard_map/dot_general | solution.py:104
  361.0 0.0 copy-done.2
  361.0 0.0 copy-done.10
  361.0 6.1 %convolution_convert_fusion.2 = bf16[1024,688]{0,1:T(8,128)(2,1)} fusion(bf16[1024,1024]{1,0:T(8,128)(2,1)S(1)} %copy-done.2, bf16[1024,688]{0,1:T(8,128)(2,1)S(1)} %copy-done.10, f32[1024,1377]{0,1:T(8,128)} %all-reduce.3.cloned.1.call-done, f32[1024]{0:T(1024)S(1)} %bitcast.33), kind=kOutput, calls=%fused_computation.15 | convolution fusion | flops 1453408256 | bytes 10555392 | tf_op jit(solution)/shard_map/dot_general | solution.py:101
  367.1 0.0 all-to-all-done.4
  367.1 0.4 convert_reduce_fusion
  367.4 1.5 add_convert_fusion
  (13 shorter events, 0.1 us)
Async XLA Ops:
  7.2 234.6 %copy-start = (bf16[688,1024]{1,0:T(8,128)(2,1)S(1)}, bf16[688,1024]{1,0:T(8,128)(2,1)}, u32[]{:S(2)}) copy-start(bf16[688,1024]{1,0:T(8,128)(2,1)} %param.18) | copy-start | bytes 4227076
  12.1 26.3 %all-to-all-start = ((bf16[32,4,1024]{2,1,0:T(4,128)(2,1)}), bf16[32,4,1024]{2,1,0:T(4,128)(2,1)S(1)}, u32[]{:S(2)}, u32[]{:S(2)}) async-start(bf16[32,4,1024]{2,1,0:T(4,128)(2,1)} %all_to_all.23), calls=%async_computation | async-start | bytes 524288 | tf_op jit(solution)/shard_map/all_to_all | solution.py:41
  38.7 9.1 %copy-start.4 = (bf16[32,1024]{1,0:T(8,128)(2,1)}, bf16[32,1024]{1,0:T(8,128)(2,1)S(1)}, u32[]{:S(2)}) copy-start(bf16[32,1024]{1,0:T(8,128)(2,1)S(1)} %convolution_convert_fusion.6) | copy-start | bytes 196612
  65.7 6.8 %copy-start.5 = (bf16[1024]{0:T(1024)(128)(2,1)S(1)}, bf16[1024]{0:T(1024)(128)(2,1)}, u32[]{:S(2)}) copy-start(bf16[1024]{0:T(1024)(128)(2,1)} %param.15) | copy-start | bytes 6148
  67.3 22.5 %all-to-all-start.3 = ((bf16[4,256,1024]{2,1,0:T(8,128)(2,1)}), bf16[4,256,1024]{2,1,0:T(8,128)(2,1)S(1)}, u32[]{:S(2)}, u32[]{:S(2)}) async-start(bf16[4,256,1024]{2,1,0:T(8,128)(2,1)} %stack.15), calls=%async_computation.3 | async-start | bytes 4194304 | tf_op jit(solution)/shard_map/all_to_all | solution.py:52
  72.4 165.1 %all-reduce.3.cloned.1.call-start = ((), (), s32[]{:S(2)}) async-start(), calls=%async_computation.5 | async-start | bytes 11337728 | tf_op jit(solution)/shard_map/psum | solution.py:61
  89.8 1.4 copy-start.8
  91.2 1.7 copy-start.1
  91.2 2.1 copy-start.9
  241.8 3.2 copy-start.3
  245.0 10.3 %copy-start.6 = (s32[32]{0:T(128)S(1)}, s32[32]{0:T(128)}, u32[]{:S(2)}) copy-start(s32[32]{0:T(128)} %param.13) | copy-start | bytes 388
  245.0 10.5 %copy-start.7 = (s32[32]{0:T(128)S(1)}, s32[32]{0:T(128)}, u32[]{:S(2)}) copy-start(s32[32]{0:T(128)} %param.14) | copy-start | bytes 388
  245.0 122.1 %all-to-all-start.4 = ((bf16[32,32,1024]{2,1,0:T(8,128)(2,1)}), bf16[32,32,1024]{2,1,0:T(8,128)(2,1)S(1)}, u32[]{:S(2)}, u32[]{:S(2)}) async-start(bf16[32,32,1024]{2,1,0:T(8,128)(2,1)} %bitcast.28), calls=%async_computation.4 | async-start | bytes 4194304 | tf_op jit(solution)/shard_map/all_to_all | solution.py:70
  255.0 100.0 %all-reduce.5.cloned.1.call-start = ((), (), s32[]{:S(2)}) async-start(), calls=%async_computation.6 | async-start | bytes 2818048 | tf_op jit(solution)/shard_map/psum | solution.py:91
  355.0 5.9 %copy-start.2 = (bf16[1024,1024]{1,0:T(8,128)(2,1)S(1)}, bf16[1024,1024]{1,0:T(8,128)(2,1)}, u32[]{:S(2)}) copy-start(bf16[1024,1024]{1,0:T(8,128)(2,1)} %copy-done.1) | copy-start | bytes 6291460
  355.0 5.9 %copy-start.10 = (bf16[1024,688]{0,1:T(8,128)(2,1)S(1)}, bf16[1024,688]{0,1:T(8,128)(2,1)}, u32[]{:S(2)}) copy-start(bf16[1024,688]{0,1:T(8,128)(2,1)} %all-reduce.5.cloned.1.call-done) | copy-start | bytes 4227076
Sparse Core Ops, SparseCore 0:
  98.7 138.8 all-reduce.2
  261.5 93.5 all-reduce.4
